TPU v7x, 1024 devices: a whole 8x8x8 slice. The times are simulated.
1024 devices in a mesh: batch: 8 (over z), seq: 8 (over x), head: 16 (over y, core).
Axes of the slice: x: 8, y: 8, z: 8, core: 2. Of those that a mesh axis runs over, the one named last changes fastest.
Arguments:
- queries: bfloat16 [40960, 8192], P(('batch', 'seq', 'head')), parts along dimension 0, may hold values from -6 to 6
- keys: bfloat16 [40960, 8192], P(('batch', 'seq', 'head')), parts along dimension 0, may hold values from -6 to 6
- values: bfloat16 [40960, 8192], P(('batch', 'seq', 'head')), parts along dimension 0, may hold values from -6 to 6
- group_order: int32 [64, 2], P(('batch', 'seq')), parts along dimension 0, may hold values from 0 to 15, as said below
- gain: float32 [8192], P('head'), may hold values from 0.1 to 1.9
Outputs:
- attended: bfloat16 [40960, 8192], P(('batch', 'seq'), 'head'), parts along dimension 0
There are 8 independent parts, one for each index of `batch`. A program takes and returns all parts, laid end to end along the dimension named above; an argument that names none is the same for every part. Nothing has to cross between parts.
Inputs may be any that keep to these rules, and one draw needn't show every extreme that they name: `group_order`: row d holds d and 15 - d, in either order.
All inputs are finite; a program needn't handle non-finite values.
Results may differ from a plain program's by a relative error of at most 0.01.
Values may be sent and summed in bfloat16 or wider, within the bound.
No kernel may reach another device: no remote copies, remote signals or barrier semaphores. Data moves between devices by JAX's collectives and lax.ppermute only.
A program may use at most 32 MiB of HBM per device.

v0:
```python
import jax
import jax.numpy as jnp
from jax import lax
from jax.sharding import PartitionSpec as P

DH = 128


def exchange(lows, both, here, pairs):
    low_sum = jnp.zeros(lows.shape, jnp.float32)
    high_sum = jnp.zeros(lows.shape, jnp.float32)
    for shift in range(1, pairs):
        src = (here - shift) % pairs
        to = (here + shift) % pairs
        msg = jnp.where(to > here, lows, both)
        got = lax.ppermute(
            msg, "seq", [(i, (i + shift) % pairs) for i in range(pairs)]
        ).astype(jnp.float32)
        low_sum = low_sum + jnp.where(src < here, got, 0.0)
        high_sum = high_sum + got
    return low_sum, high_sum


def local(queries, keys, values, group_order, gain):
    rows_in, feats = keys.shape
    ndev = lax.axis_size("head")
    width = feats // ndev
    local_heads = gain.shape[0] // DH
    groups = 2
    gh = local_heads // groups
    rows = ndev * rows_in
    half = rows // 2
    pairs = lax.axis_size("seq")
    here = lax.axis_index("seq")
    order = group_order[0]
    low_first = order[0] < pairs

    def by_dest(x):
        return x.reshape(rows_in, ndev, width).transpose(1, 0, 2)

    kd = by_dest(keys).reshape(ndev, rows_in, groups, gh * DH)
    vd = by_dest(values).reshape(ndev, rows_in, groups, gh * DH)
    tie = ()
    kx_parts, vx_parts, pre_parts = [], [], []
    for g in range(groups):
        kv = jnp.stack([kd[:, :, g], vd[:, :, g]], axis=1).reshape(ndev, 2 * rows_in, gh * DH)
        if tie:
            kv, tie = lax.optimization_barrier((kv, tie))
            pre_parts.append(exchange(*tie, here, pairs))
        kv_all = lax.all_to_all(kv, "head", split_axis=0, concat_axis=0, tiled=True)
        kv_all = kv_all.reshape(ndev, 2, rows_in, gh * DH)
        kx = kv_all[:, 0].reshape(rows, gh, DH)
        vx = kv_all[:, 1].reshape(rows, gh, DH)
        kx_parts.append(kx)
        vx_parts.append(vx)
        kh = kx.reshape(2, half, gh, DH)
        vh = vx.reshape(2, half, gh, DH)
        state = jnp.einsum("jthd,jthe->jhde", kh, vh, preferred_element_type=jnp.float32).astype(
            jnp.bfloat16
        )
        lows = jnp.where(low_first, state[0], state[1])
        highs = jnp.where(low_first, state[1], state[0])
        both = (lows.astype(jnp.float32) + highs.astype(jnp.float32)).astype(jnp.bfloat16)
        tie = (lows, both)
    q_in, tie = lax.optimization_barrier((by_dest(queries), tie))
    pre_parts.append(exchange(*tie, here, pairs))
    q_all = lax.all_to_all(q_in, "head", split_axis=0, concat_axis=0, tiled=True)
    qx = q_all.reshape(rows, local_heads, DH)
    kx = jnp.concatenate(kx_parts, axis=1)
    vx = jnp.concatenate(vx_parts, axis=1)
    low_sum = jnp.concatenate([p[0] for p in pre_parts], axis=0)
    high_sum = jnp.concatenate([p[1] for p in pre_parts], axis=0)
    first_pre = jnp.where(low_first, low_sum, high_sum).astype(jnp.bfloat16)
    second_pre = jnp.where(low_first, high_sum, low_sum).astype(jnp.bfloat16)
    index = jnp.arange(rows, dtype=jnp.int32)
    position = order[index // half] * half + index % half
    scores = jnp.einsum("thd,shd->hts", qx, kx, preferred_element_type=jnp.float32)
    allowed = position[:, None] >= position[None, :]
    scores = jnp.where(allowed[None], scores, 0.0).astype(jnp.bfloat16)
    intra = jnp.einsum("hts,she->the", scores, vx, preferred_element_type=jnp.float32)
    qh = qx.reshape(2, half, local_heads, DH)
    first_term = jnp.einsum("thd,hde->the", qh[0], first_pre, preferred_element_type=jnp.float32)
    second_term = jnp.einsum("thd,hde->the", qh[1], second_pre, preferred_element_type=jnp.float32)
    raw = intra + jnp.concatenate([first_term, second_term], axis=0)
    scale = lax.rsqrt(jnp.mean(raw * raw, axis=-1, keepdims=True) + 1e-06)
    gains = gain.reshape(local_heads, DH)
    return (raw * scale * gains).astype(jnp.bfloat16).reshape(rows, local_heads * DH)


def solution(mesh):
    return jax.shard_map(
        local,
        mesh=mesh,
        in_specs=(
            P(("batch", "seq", "head"), None),
            P(("batch", "seq", "head"), None),
            P(("batch", "seq", "head"), None),
            P(("batch", "seq"), None),
            P("head"),
        ),
        out_specs=P(("batch", "seq"), "head"),
        check_vma=False,
    )
```

profile of v0, /device:TPU:18, one launch (start us, length us, event | category | flops | bytes accessed | tf_op | source)
XLA Modules:
  0.0 137.3 jit_solution(17671198130368948871)
XLA Ops:
  0.0 1.2 copy.96
  1.6 0.9 fusion.55
  2.5 0.9 fusion.54
  4.6 7.9 %all-to-all-start = ((bf16[16,80,256]{2,1,0:T(8,128)(2,1)}), bf16[16,80,256]{2,1,0:T(8,128)(2,1)S(1)}, u32[]{:S(2)}, u32[]{:S(2)}) async-start(bf16[16,80,256]{2,1,0:T(8,128)(2,1)} %bitcast.2), calls=%async_computation | async-start | bytes 1310720 | tf_op jit(solution)/shard_map/all_to_all | solution.py:50
  12.6 0.9 copy.45
  14.8 14.3 %all-to-all-done = bf16[16,80,256]{2,1,0:T(8,128)(2,1)S(1)} async-done(((bf16[16,80,256]{2,1,0:T(8,128)(2,1)}), bf16[16,80,256]{2,1,0:T(8,128)(2,1)S(1)}, u32[]{:S(2)}, u32[]{:S(2)}) %all-to-all-start) | async-done | bytes 655392 | tf_op jit(solution)/shard_map/all_to_all | solution.py:50
  29.7 6.5 %all-to-all-start.1 = ((bf16[16,80,256]{2,1,0:T(8,128)(2,1)}), bf16[16,80,256]{2,1,0:T(8,128)(2,1)S(1)}, u32[]{:S(2)}, u32[]{:S(2)}) async-start(bf16[16,80,256]{2,1,0:T(8,128)(2,1)} %bitcast.4), calls=%async_computation.1 | async-start | bytes 1310720 | tf_op jit(solution)/shard_map/all_to_all | solution.py:50
  37.0 1.3 fusion.45
  38.3 14.5 %all-to-all-done.1 = bf16[16,80,256]{2,1,0:T(8,128)(2,1)S(1)} async-done(((bf16[16,80,256]{2,1,0:T(8,128)(2,1)}), bf16[16,80,256]{2,1,0:T(8,128)(2,1)S(1)}, u32[]{:S(2)}, u32[]{:S(2)}) %all-to-all-start.1) | async-done | bytes 655392 | tf_op jit(solution)/shard_map/all_to_all | solution.py:50
  53.4 6.3 %all-to-all-start.2 = ((bf16[16,40,512]{2,1,0:T(8,128)(2,1)}), bf16[16,40,512]{2,1,0:T(8,128)(2,1)S(1)}, u32[]{:S(2)}, u32[]{:S(2)}) async-start(bf16[16,40,512]{2,1,0:T(8,128)(2,1)} %bitcast.69), calls=%async_computation.2 | async-start | bytes 1310720 | tf_op jit(solution)/shard_map/all_to_all | solution.py:67
  59.9 3.4 %collective-permute-start = (bf16[2,128,128]{2,1,0:T(8,128)(2,1)S(1)}, bf16[2,128,128]{2,1,0:T(8,128)(2,1)S(1)}, u32[]{:S(2)}, u32[]{:S(2)}) collective-permute-start(bf16[2,128,128]{2,1,0:T(8,128)(2,1)S(1)} %get-tuple-element.35), channel_id=1, source_target_pairs={{0,16},{16,32},{32,48},{48,64},{64,80},{80,96},{96,112},{112,0},{1... | collective-permute-start | bytes 196616 | tf_op jit(solution)/shard_map/ppermute | solution.py:16
  63.3 9.4 %collective-permute-start.6 = (bf16[2,128,128]{2,1,0:T(8,128)(2,1)S(1)}, bf16[2,128,128]{2,1,0:T(8,128)(2,1)S(1)}, u32[]{:S(2)}, u32[]{:S(2)}) collective-permute-start(bf16[2,128,128]{2,1,0:T(8,128)(2,1)S(1)} %get-tuple-element.36), channel_id=1, source_target_pairs={{0,112},{16,0},{32,16},{48,32},{64,48},{80,64},{96,80},{112,96},{1... | collective-permute-start | bytes 196616 | tf_op jit(solution)/shard_map/ppermute | solution.py:16
  72.8 4.6 %collective-permute-start.5 = (bf16[2,128,128]{2,1,0:T(8,128)(2,1)S(1)}, bf16[2,128,128]{2,1,0:T(8,128)(2,1)S(1)}, u32[]{:S(2)}, u32[]{:S(2)}) collective-permute-start(bf16[2,128,128]{2,1,0:T(8,128)(2,1)S(1)} %get-tuple-element.37), channel_id=1, source_target_pairs={{0,96},{16,112},{32,0},{48,16},{64,32},{80,48},{96,64},{112,80},{1... | collective-permute-start | bytes 196616 | tf_op jit(solution)/shard_map/ppermute | solution.py:16
  77.4 1.9 %collective-permute-start.4 = (bf16[2,128,128]{2,1,0:T(8,128)(2,1)S(1)}, bf16[2,128,128]{2,1,0:T(8,128)(2,1)S(1)}, u32[]{:S(2)}, u32[]{:S(2)}) collective-permute-start(bf16[2,128,128]{2,1,0:T(8,128)(2,1)S(1)} %get-tuple-element.38), channel_id=1, source_target_pairs={{0,80},{16,96},{32,112},{48,0},{64,16},{80,32},{96,48},{112,64},{1... | collective-permute-start | bytes 196616 | tf_op jit(solution)/shard_map/ppermute | solution.py:16
  79.3 8.4 %collective-permute-start.3 = (bf16[2,128,128]{2,1,0:T(8,128)(2,1)S(1)}, bf16[2,128,128]{2,1,0:T(8,128)(2,1)S(1)}, u32[]{:S(2)}, u32[]{:S(2)}) collective-permute-start(bf16[2,128,128]{2,1,0:T(8,128)(2,1)S(1)} %get-tuple-element.39), channel_id=1, source_target_pairs={{0,64},{16,80},{32,96},{48,112},{64,0},{80,16},{96,32},{112,48},{1... | collective-permute-start | bytes 196616 | tf_op jit(solution)/shard_map/ppermute | solution.py:16
  87.7 1.9 %collective-permute-start.2 = (bf16[2,128,128]{2,1,0:T(8,128)(2,1)S(1)}, bf16[2,128,128]{2,1,0:T(8,128)(2,1)S(1)}, u32[]{:S(2)}, u32[]{:S(2)}) collective-permute-start(bf16[2,128,128]{2,1,0:T(8,128)(2,1)S(1)} %get-tuple-element.40), channel_id=1, source_target_pairs={{0,48},{16,64},{32,80},{48,96},{64,112},{80,0},{96,16},{112,32},{1... | collective-permute-start | bytes 196616 | tf_op jit(solution)/shard_map/ppermute | solution.py:16
  89.7 3.4 %collective-permute-start.1 = (bf16[2,128,128]{2,1,0:T(8,128)(2,1)S(1)}, bf16[2,128,128]{2,1,0:T(8,128)(2,1)S(1)}, u32[]{:S(2)}, u32[]{:S(2)}) collective-permute-start(bf16[2,128,128]{2,1,0:T(8,128)(2,1)S(1)} %get-tuple-element.41), channel_id=1, source_target_pairs={{0,32},{16,48},{32,64},{48,80},{64,96},{80,112},{96,0},{112,16},{1... | collective-permute-start | bytes 196616 | tf_op jit(solution)/shard_map/ppermute | solution.py:16
  93.1 3.4 %collective-permute-start.7 = (bf16[2,128,128]{2,1,0:T(8,128)(2,1)S(1)}, bf16[2,128,128]{2,1,0:T(8,128)(2,1)S(1)}, u32[]{:S(2)}, u32[]{:S(2)}) collective-permute-start(bf16[2,128,128]{2,1,0:T(8,128)(2,1)S(1)} %get-tuple-element.42), channel_id=1, source_target_pairs={{0,16},{16,32},{32,48},{48,64},{64,80},{80,96},{96,112},{112,0},{1... | collective-permute-start | bytes 196616 | tf_op jit(solution)/shard_map/ppermute | solution.py:16
  96.4 2.5 %collective-permute-start.13 = (bf16[2,128,128]{2,1,0:T(8,128)(2,1)S(1)}, bf16[2,128,128]{2,1,0:T(8,128)(2,1)S(1)}, u32[]{:S(2)}, u32[]{:S(2)}) collective-permute-start(bf16[2,128,128]{2,1,0:T(8,128)(2,1)S(1)} %get-tuple-element.43), channel_id=1, source_target_pairs={{0,112},{16,0},{32,16},{48,32},{64,48},{80,64},{96,80},{112,96},{1... | collective-permute-start | bytes 196616 | tf_op jit(solution)/shard_map/ppermute | solution.py:16
  98.9 1.0 broadcast_compare_fusion
  100.9 1.4 %copy.48 = bf16[640,2,128]{0,2,1:T(8,128)(2,1)} copy(bf16[640,2,128]{2,1,0:T(2,128)(2,1)S(1)} %reshape_squeeze.12) | data formatting | bytes 655360 | tf_op jit(solution)/shard_map/reshape;squeeze | solution.py:53
  102.4 4.6 %collective-permute-start.12 = (bf16[2,128,128]{2,1,0:T(8,128)(2,1)S(1)}, bf16[2,128,128]{2,1,0:T(8,128)(2,1)S(1)}, u32[]{:S(2)}, u32[]{:S(2)}) collective-permute-start(bf16[2,128,128]{2,1,0:T(8,128)(2,1)S(1)} %get-tuple-element.44), channel_id=1, source_target_pairs={{0,96},{16,112},{32,0},{48,16},{64,32},{80,48},{96,64},{112,80},{1... | collective-permute-start | bytes 196616 | tf_op jit(solution)/shard_map/ppermute | solution.py:16
  106.9 6.9 %collective-permute-start.11 = (bf16[2,128,128]{2,1,0:T(8,128)(2,1)S(1)}, bf16[2,128,128]{2,1,0:T(8,128)(2,1)S(1)}, u32[]{:S(2)}, u32[]{:S(2)}) collective-permute-start(bf16[2,128,128]{2,1,0:T(8,128)(2,1)S(1)} %get-tuple-element.45), channel_id=1, source_target_pairs={{0,80},{16,96},{32,112},{48,0},{64,16},{80,32},{96,48},{112,64},{1... | collective-permute-start | bytes 196616 | tf_op jit(solution)/shard_map/ppermute | solution.py:16
  113.9 1.9 %collective-permute-start.10 = (bf16[2,128,128]{2,1,0:T(8,128)(2,1)S(1)}, bf16[2,128,128]{2,1,0:T(8,128)(2,1)S(1)}, u32[]{:S(2)}, u32[]{:S(2)}) collective-permute-start(bf16[2,128,128]{2,1,0:T(8,128)(2,1)S(1)} %get-tuple-element.46), channel_id=1, source_target_pairs={{0,64},{16,80},{32,96},{48,112},{64,0},{80,16},{96,32},{112,48},{1... | collective-permute-start | bytes 196616 | tf_op jit(solution)/shard_map/ppermute | solution.py:16
  115.8 6.4 %collective-permute-start.9 = (bf16[2,128,128]{2,1,0:T(8,128)(2,1)S(1)}, bf16[2,128,128]{2,1,0:T(8,128)(2,1)S(1)}, u32[]{:S(2)}, u32[]{:S(2)}) collective-permute-start(bf16[2,128,128]{2,1,0:T(8,128)(2,1)S(1)} %get-tuple-element.47), channel_id=1, source_target_pairs={{0,48},{16,64},{32,80},{48,96},{64,112},{80,0},{96,16},{112,32},{1... | collective-permute-start | bytes 196616 | tf_op jit(solution)/shard_map/ppermute | solution.py:16
  122.2 2.2 %collective-permute-start.8 = (bf16[2,128,128]{2,1,0:T(8,128)(2,1)S(1)}, bf16[2,128,128]{2,1,0:T(8,128)(2,1)S(1)}, u32[]{:S(2)}, u32[]{:S(2)}) collective-permute-start(bf16[2,128,128]{2,1,0:T(8,128)(2,1)S(1)} %get-tuple-element.48), channel_id=1, source_target_pairs={{0,32},{16,48},{32,64},{48,80},{64,96},{80,112},{96,0},{112,16},{1... | collective-permute-start | bytes 196616 | tf_op jit(solution)/shard_map/ppermute | solution.py:16
  125.5 1.4 %copy.49 = bf16[640,2,128]{0,2,1:T(8,128)(2,1)} copy(bf16[640,2,128]{2,1,0:T(2,128)(2,1)S(1)} %reshape_squeeze.13) | data formatting | bytes 655360 | tf_op jit(solution)/shard_map/reshape;squeeze | solution.py:53
  126.9 1.0 collective-permute-done.9
  127.9 2.7 %collective-permute-done.8 = bf16[2,128,128]{2,1,0:T(8,128)(2,1)S(1)} collective-permute-done((bf16[2,128,128]{2,1,0:T(8,128)(2,1)S(1)}, bf16[2,128,128]{2,1,0:T(8,128)(2,1)S(1)}, u32[]{:S(2)}, u32[]{:S(2)}) %collective-permute-start.8) | collective-permute-done | bytes 65568 | tf_op jit(solution)/shard_map/ppermute | solution.py:16
  131.3 1.2 convolution_bitcast_fusion.1
  132.6 3.4 %multiply_reduce_fusion = (f32[640,4]{0,1:T(4,128)S(1)}, f32[640,4,128]{0,2,1:T(8,128)S(1)}) fusion(f32[320,4,128]{0,2,1:T(8,128)S(1)} %convolution_bitcast_fusion, f32[320,4,128]{0,2,1:T(8,128)S(1)} %convolution_bitcast_fusion.1, pred[640,640]{1,0:T(8,128)(4,1)} %broadcast_compare_fusion, bf16[640,2,128]{2,0,1:T(8,128)(2,1)} %copy.54, ...), kind=kOutput, calls=%fused_computation.8 | convolution fusion | flops 844101120 | bytes 5007360 | tf_op jit(solution)/shard_map/hts,she->the/dot_general | solution.py:80
  136.2 1.1 copy.60
  (63 shorter events, 7.3 us)
Async XLA Ops:
  0.0 1.4 copy-start
  4.6 24.4 %all-to-all-start = ((bf16[16,80,256]{2,1,0:T(8,128)(2,1)}), bf16[16,80,256]{2,1,0:T(8,128)(2,1)S(1)}, u32[]{:S(2)}, u32[]{:S(2)}) async-start(bf16[16,80,256]{2,1,0:T(8,128)(2,1)} %bitcast.2), calls=%async_computation | async-start | bytes 1310720 | tf_op jit(solution)/shard_map/all_to_all | solution.py:50
  12.5 1.0 copy-start.4
  29.3 6.9 %copy-start.1 = (bf16[40,8192]{1,0:T(8,128)(2,1)S(1)}, bf16[40,8192]{1,0:T(8,128)(2,1)}, u32[]{:S(2)}) copy-start(bf16[40,8192]{1,0:T(8,128)(2,1)} %param.5) | copy-start | bytes 1966084
  29.7 23.2 %all-to-all-start.1 = ((bf16[16,80,256]{2,1,0:T(8,128)(2,1)}), bf16[16,80,256]{2,1,0:T(8,128)(2,1)S(1)}, u32[]{:S(2)}, u32[]{:S(2)}) async-start(bf16[16,80,256]{2,1,0:T(8,128)(2,1)} %bitcast.4), calls=%async_computation.1 | async-start | bytes 1310720 | tf_op jit(solution)/shard_map/all_to_all | solution.py:50
  53.4 77.2 %all-to-all-start.2 = ((bf16[16,40,512]{2,1,0:T(8,128)(2,1)}), bf16[16,40,512]{2,1,0:T(8,128)(2,1)S(1)}, u32[]{:S(2)}, u32[]{:S(2)}) async-start(bf16[16,40,512]{2,1,0:T(8,128)(2,1)} %bitcast.69), calls=%async_computation.2 | async-start | bytes 1310720 | tf_op jit(solution)/shard_map/all_to_all | solution.py:67
  59.9 27.8 %collective-permute-start = (bf16[2,128,128]{2,1,0:T(8,128)(2,1)S(1)}, bf16[2,128,128]{2,1,0:T(8,128)(2,1)S(1)}, u32[]{:S(2)}, u32[]{:S(2)}) collective-permute-start(bf16[2,128,128]{2,1,0:T(8,128)(2,1)S(1)} %get-tuple-element.35), channel_id=1, source_target_pairs={{0,16},{16,32},{32,48},{48,64},{64,80},{80,96},{96,112},{112,0},{1... | collective-permute-start | bytes 196616 | tf_op jit(solution)/shard_map/ppermute | solution.py:16
  63.3 26.4 %collective-permute-start.6 = (bf16[2,128,128]{2,1,0:T(8,128)(2,1)S(1)}, bf16[2,128,128]{2,1,0:T(8,128)(2,1)S(1)}, u32[]{:S(2)}, u32[]{:S(2)}) collective-permute-start(bf16[2,128,128]{2,1,0:T(8,128)(2,1)S(1)} %get-tuple-element.36), channel_id=1, source_target_pairs={{0,112},{16,0},{32,16},{48,32},{64,48},{80,64},{96,80},{112,96},{1... | collective-permute-start | bytes 196616 | tf_op jit(solution)/shard_map/ppermute | solution.py:16
  72.8 20.3 %collective-permute-start.5 = (bf16[2,128,128]{2,1,0:T(8,128)(2,1)S(1)}, bf16[2,128,128]{2,1,0:T(8,128)(2,1)S(1)}, u32[]{:S(2)}, u32[]{:S(2)}) collective-permute-start(bf16[2,128,128]{2,1,0:T(8,128)(2,1)S(1)} %get-tuple-element.37), channel_id=1, source_target_pairs={{0,96},{16,112},{32,0},{48,16},{64,32},{80,48},{96,64},{112,80},{1... | collective-permute-start | bytes 196616 | tf_op jit(solution)/shard_map/ppermute | solution.py:16
  77.4 19.1 %collective-permute-start.4 = (bf16[2,128,128]{2,1,0:T(8,128)(2,1)S(1)}, bf16[2,128,128]{2,1,0:T(8,128)(2,1)S(1)}, u32[]{:S(2)}, u32[]{:S(2)}) collective-permute-start(bf16[2,128,128]{2,1,0:T(8,128)(2,1)S(1)} %get-tuple-element.38), channel_id=1, source_target_pairs={{0,80},{16,96},{32,112},{48,0},{64,16},{80,32},{96,48},{112,64},{1... | collective-permute-start | bytes 196616 | tf_op jit(solution)/shard_map/ppermute | solution.py:16
  79.3 23.1 %collective-permute-start.3 = (bf16[2,128,128]{2,1,0:T(8,128)(2,1)S(1)}, bf16[2,128,128]{2,1,0:T(8,128)(2,1)S(1)}, u32[]{:S(2)}, u32[]{:S(2)}) collective-permute-start(bf16[2,128,128]{2,1,0:T(8,128)(2,1)S(1)} %get-tuple-element.39), channel_id=1, source_target_pairs={{0,64},{16,80},{32,96},{48,112},{64,0},{80,16},{96,32},{112,48},{1... | collective-permute-start | bytes 196616 | tf_op jit(solution)/shard_map/ppermute | solution.py:16
  87.7 19.2 %collective-permute-start.2 = (bf16[2,128,128]{2,1,0:T(8,128)(2,1)S(1)}, bf16[2,128,128]{2,1,0:T(8,128)(2,1)S(1)}, u32[]{:S(2)}, u32[]{:S(2)}) collective-permute-start(bf16[2,128,128]{2,1,0:T(8,128)(2,1)S(1)} %get-tuple-element.40), channel_id=1, source_target_pairs={{0,48},{16,64},{32,80},{48,96},{64,112},{80,0},{96,16},{112,32},{1... | collective-permute-start | bytes 196616 | tf_op jit(solution)/shard_map/ppermute | solution.py:16
  89.7 24.2 %collective-permute-start.1 = (bf16[2,128,128]{2,1,0:T(8,128)(2,1)S(1)}, bf16[2,128,128]{2,1,0:T(8,128)(2,1)S(1)}, u32[]{:S(2)}, u32[]{:S(2)}) collective-permute-start(bf16[2,128,128]{2,1,0:T(8,128)(2,1)S(1)} %get-tuple-element.41), channel_id=1, source_target_pairs={{0,32},{16,48},{32,64},{48,80},{64,96},{80,112},{96,0},{112,16},{1... | collective-permute-start | bytes 196616 | tf_op jit(solution)/shard_map/ppermute | solution.py:16
  93.1 22.8 %collective-permute-start.7 = (bf16[2,128,128]{2,1,0:T(8,128)(2,1)S(1)}, bf16[2,128,128]{2,1,0:T(8,128)(2,1)S(1)}, u32[]{:S(2)}, u32[]{:S(2)}) collective-permute-start(bf16[2,128,128]{2,1,0:T(8,128)(2,1)S(1)} %get-tuple-element.42), channel_id=1, source_target_pairs={{0,16},{16,32},{32,48},{48,64},{64,80},{80,96},{96,112},{112,0},{1... | collective-permute-start | bytes 196616 | tf_op jit(solution)/shard_map/ppermute | solution.py:16
  96.4 25.8 %collective-permute-start.13 = (bf16[2,128,128]{2,1,0:T(8,128)(2,1)S(1)}, bf16[2,128,128]{2,1,0:T(8,128)(2,1)S(1)}, u32[]{:S(2)}, u32[]{:S(2)}) collective-permute-start(bf16[2,128,128]{2,1,0:T(8,128)(2,1)S(1)} %get-tuple-element.43), channel_id=1, source_target_pairs={{0,112},{16,0},{32,16},{48,32},{64,48},{80,64},{96,80},{112,96},{1... | collective-permute-start | bytes 196616 | tf_op jit(solution)/shard_map/ppermute | solution.py:16
  102.4 24.6 %collective-permute-start.12 = (bf16[2,128,128]{2,1,0:T(8,128)(2,1)S(1)}, bf16[2,128,128]{2,1,0:T(8,128)(2,1)S(1)}, u32[]{:S(2)}, u32[]{:S(2)}) collective-permute-start(bf16[2,128,128]{2,1,0:T(8,128)(2,1)S(1)} %get-tuple-element.44), channel_id=1, source_target_pairs={{0,96},{16,112},{32,0},{48,16},{64,32},{80,48},{96,64},{112,80},{1... | collective-permute-start | bytes 196616 | tf_op jit(solution)/shard_map/ppermute | solution.py:16
  106.9 20.0 %collective-permute-start.11 = (bf16[2,128,128]{2,1,0:T(8,128)(2,1)S(1)}, bf16[2,128,128]{2,1,0:T(8,128)(2,1)S(1)}, u32[]{:S(2)}, u32[]{:S(2)}) collective-permute-start(bf16[2,128,128]{2,1,0:T(8,128)(2,1)S(1)} %get-tuple-element.45), channel_id=1, source_target_pairs={{0,80},{16,96},{32,112},{48,0},{64,16},{80,32},{96,48},{112,64},{1... | collective-permute-start | bytes 196616 | tf_op jit(solution)/shard_map/ppermute | solution.py:16
  113.9 13.0 %collective-permute-start.10 = (bf16[2,128,128]{2,1,0:T(8,128)(2,1)S(1)}, bf16[2,128,128]{2,1,0:T(8,128)(2,1)S(1)}, u32[]{:S(2)}, u32[]{:S(2)}) collective-permute-start(bf16[2,128,128]{2,1,0:T(8,128)(2,1)S(1)} %get-tuple-element.46), channel_id=1, source_target_pairs={{0,64},{16,80},{32,96},{48,112},{64,0},{80,16},{96,32},{112,48},{1... | collective-permute-start | bytes 196616 | tf_op jit(solution)/shard_map/ppermute | solution.py:16
  115.8 12.1 %collective-permute-start.9 = (bf16[2,128,128]{2,1,0:T(8,128)(2,1)S(1)}, bf16[2,128,128]{2,1,0:T(8,128)(2,1)S(1)}, u32[]{:S(2)}, u32[]{:S(2)}) collective-permute-start(bf16[2,128,128]{2,1,0:T(8,128)(2,1)S(1)} %get-tuple-element.47), channel_id=1, source_target_pairs={{0,48},{16,64},{32,80},{48,96},{64,112},{80,0},{96,16},{112,32},{1... | collective-permute-start | bytes 196616 | tf_op jit(solution)/shard_map/ppermute | solution.py:16
  122.2 8.3 %collective-permute-start.8 = (bf16[2,128,128]{2,1,0:T(8,128)(2,1)S(1)}, bf16[2,128,128]{2,1,0:T(8,128)(2,1)S(1)}, u32[]{:S(2)}, u32[]{:S(2)}) collective-permute-start(bf16[2,128,128]{2,1,0:T(8,128)(2,1)S(1)} %get-tuple-element.48), channel_id=1, source_target_pairs={{0,32},{16,48},{32,64},{48,80},{64,96},{80,112},{96,0},{112,16},{1... | collective-permute-start | bytes 196616 | tf_op jit(solution)/shard_map/ppermute | solution.py:16
  124.5 6.4 %copy-start.2 = (bf16[2,128,128]{2,1,0:T(8,128)(2,1)}, bf16[2,128,128]{2,1,0:T(8,128)(2,1)S(1)}, u32[]{:S(2)}) copy-start(bf16[2,128,128]{2,1,0:T(8,128)(2,1)S(1)} %get-tuple-element.31) | copy-start | bytes 196612
  124.5 6.4 %copy-start.3 = (bf16[2,128,128]{2,1,0:T(8,128)(2,1)}, bf16[2,128,128]{2,1,0:T(8,128)(2,1)S(1)}, u32[]{:S(2)}) copy-start(bf16[2,128,128]{2,1,0:T(8,128)(2,1)S(1)} %get-tuple-element.32) | copy-start | bytes 196612
  132.6 3.4 %copy-start.5 = (f32[512]{0:T(512)S(1)}, f32[512]{0:T(512)}, u32[]{:S(2)}) copy-start(f32[512]{0:T(512)} %param.9) | copy-start | bytes 6148
where the time goes:
time: 138 us; the launch traced here: 137 us
  starting transfers between devices  81.5 us (59%)
  waiting for transfers between devices  32.4 us (23%)
  local copies, waits for them, and re-layouts  13.4 us (10%)
  matrix products  5.59 us (4%)
  other arithmetic  3.04 us (2%)
    ppermute x14, starting transfers between devices, exchange(): lax.ppermute(msg, 'seq', [(i, (i + shift) % pairs) for i in range(pairs)])  60.8 us
    all_to_all x2, waiting for transfers between devices, local(): kv_all = lax.all_to_all(kv, 'head', split_axis=0, concat_axis=0, tiled=True)  28.8 us
    all_to_all x2, starting transfers between devices, local(): kv_all = lax.all_to_all(kv, 'head', split_axis=0, concat_axis=0, tiled=True)  14.4 us
    all_to_all x1, starting transfers between devices, local(): lax.all_to_all(q_in, 'head', split_axis=0, concat_axis=0, tiled=True)  6.33 us
    ppermute x14, waiting for transfers between devices, exchange(): lax.ppermute(msg, 'seq', [(i, (i + shift) % pairs) for i in range(pairs)])  3.64 us
    dot_general x1, matrix products, local(): jnp.einsum('hts,she->the', scores, vx, preferred_element_type=jnp.float32)  3.4 us
    another operation x4, local copies, waits for them, and re-layouts, local(): vx = kv_all[:, 1].reshape(rows, gh, DH)  3.03 us
  transfers between devices with their start and end apart: 17, of which 4 were waited for; matrix products, arithmetic and copies ran while one was open for 7% of the time, Pallas kernels for 0%

commit v1 on v0

--- a/solution.py
+++ b/solution.py
@@ -7,17 +7,28 @@
 
 
 def exchange(lows, both, here, pairs):
-    low_sum = jnp.zeros(lows.shape, jnp.float32)
-    high_sum = jnp.zeros(lows.shape, jnp.float32)
-    for shift in range(1, pairs):
-        src = (here - shift) % pairs
-        to = (here + shift) % pairs
-        msg = jnp.where(to > here, lows, both)
-        got = lax.ppermute(
-            msg, "seq", [(i, (i + shift) % pairs) for i in range(pairs)]
-        ).astype(jnp.float32)
-        low_sum = low_sum + jnp.where(src < here, got, 0.0)
-        high_sum = high_sum + got
+    up = lows.astype(jnp.float32)
+    down = both.astype(jnp.float32)
+    step = pairs // 2
+    msg = jnp.where(here + step < pairs, lows, both)
+    got = lax.ppermute(
+        msg, "seq", [(i, (i + step) % pairs) for i in range(pairs)]
+    ).astype(jnp.float32)
+    up = up + jnp.where(here >= step, got, 0.0)
+    down = down + jnp.where(here + step < pairs, got, 0.0)
+    step //= 2
+    while step >= 1:
+        got_up = lax.ppermute(
+            up.astype(jnp.bfloat16), "seq", [(i, i + step) for i in range(pairs - step)]
+        )
+        got_down = lax.ppermute(
+            down.astype(jnp.bfloat16), "seq", [(i, i - step) for i in range(step, pairs)]
+        )
+        up = up + got_up.astype(jnp.float32)
+        down = down + got_down.astype(jnp.float32)
+        step //= 2
+    low_sum = up - lows.astype(jnp.float32)
+    high_sum = low_sum + (down - both.astype(jnp.float32))
     return low_sum, high_sum
 
 
@@ -26,7 +37,7 @@
     ndev = lax.axis_size("head")
     width = feats // ndev
     local_heads = gain.shape[0] // DH
-    groups = 2
+    groups = 1
     gh = local_heads // groups
     rows = ndev * rows_in
     half = rows // 2
@@ -78,6 +89,7 @@
     allowed = position[:, None] >= position[None, :]
     scores = jnp.where(allowed[None], scores, 0.0).astype(jnp.bfloat16)
     intra = jnp.einsum("hts,she->the", scores, vx, preferred_element_type=jnp.float32)
+    intra = lax.optimization_barrier(intra)
     qh = qx.reshape(2, half, local_heads, DH)
     first_term = jnp.einsum("thd,hde->the", qh[0], first_pre, preferred_element_type=jnp.float32)
     second_term = jnp.einsum("thd,hde->the", qh[1], second_pre, preferred_element_type=jnp.float32)

time: 138 us -> 95.4 us (0.69)
  the two profiles are of different devices: /device:TPU:18 before, /device:TPU:902 now
where the time goes in v1:
time: 95.4 us; the launch traced here: 94.9 us
  waiting for transfers between devices  42.9 us (45%)
  starting transfers between devices  34.4 us (36%)
  local copies, waits for them, and re-layouts  6.97 us (7%)
  other arithmetic  5.29 us (6%)
  matrix products  4.57 us (5%)
    all_to_all x1, waiting for transfers between devices, local(): kv_all = lax.all_to_all(kv, 'head', split_axis=0, concat_axis=0, tiled=True)  30 us
    ppermute x2, starting transfers between devices, exchange(): lax.ppermute(up.astype(jnp.bfloat16), 'seq', [(i, i + step) for i in rang...  10 us
    all_to_all x1, starting transfers between devices, local(): kv_all = lax.all_to_all(kv, 'head', split_axis=0, concat_axis=0, tiled=True)  7.79 us
    ppermute x1, waiting for transfers between devices, exchange(): lax.ppermute(msg, 'seq', [(i, (i + step) % pairs) for i in range(pairs)])  7.09 us
    ppermute x2, starting transfers between devices, exchange(): lax.ppermute(down.astype(jnp.bfloat16), 'seq', [(i, i - step) for i in ra...  6.94 us
    all_to_all x1, starting transfers between devices, local(): lax.all_to_all(q_in, 'head', split_axis=0, concat_axis=0, tiled=True)  4.93 us
    ppermute x1, starting transfers between devices, exchange(): lax.ppermute(msg, 'seq', [(i, (i + step) % pairs) for i in range(pairs)])  4.69 us
    ppermute x2, waiting for transfers between devices, exchange(): lax.ppermute(up.astype(jnp.bfloat16), 'seq', [(i, i + step) for i in rang...  3.99 us
  transfers between devices with their start and end apart: 7, of which 4 were waited for; matrix products, arithmetic and copies ran while one was open for 11% of the time, Pallas kernels for 0%

profile of v1, /device:TPU:902, one launch (start us, length us, event | category | flops | bytes accessed | tf_op | source)
XLA Modules:
  0.0 94.9 jit_solution(17382377598827235072)
XLA Ops:
  0.0 1.4 %bitcast_bitcast_fusion.1 = (bf16[16,1,40,512]{3,2,1,0:T(8,128)(2,1)S(1)}, bf16[16,1,40,512]{3,2,1,0:T(8,128)(2,1)S(1)}) fusion(bf16[5,16,8,512]{3,2,1,0:T(8,128)(2,1)} %bitcast.50, bf16[5,16,8,512]{3,2,1,0:T(8,128)(2,1)} %bitcast.51), kind=kLoop, calls=%fused_computation.15 | loop fusion | bytes 2621440 | tf_op jit(solution)/shard_map/stack;squeeze;reshape | solution.py:57
  1.4 1.2 %pad_maximum_fusion = bf16[16,2,40,512]{3,2,1,0:T(8,128)(2,1)} fusion(bf16[16,1,40,512]{3,2,1,0:T(8,128)(2,1)S(1)} %get-tuple-element.23, bf16[16,1,40,512]{3,2,1,0:T(8,128)(2,1)S(1)} %get-tuple-element.24), kind=kLoop, calls=%fused_computation.6 | loop fusion | flops 655360 | bytes 2621440 | tf_op jit(solution)/shard_map/stack | solution.py:57
  2.6 7.8 %all-to-all-start = ((bf16[16,80,512]{2,1,0:T(8,128)(2,1)}), bf16[16,80,512]{2,1,0:T(8,128)(2,1)S(1)}, u32[]{:S(2)}, u32[]{:S(2)}) async-start(bf16[16,80,512]{2,1,0:T(8,128)(2,1)} %bitcast.4), calls=%async_computation | async-start | bytes 2621440 | tf_op jit(solution)/shard_map/all_to_all | solution.py:61
  10.4 0.9 copy.46
  11.3 0.6 fusion.37
  12.5 30.0 %all-to-all-done = bf16[16,80,512]{2,1,0:T(8,128)(2,1)S(1)} async-done(((bf16[16,80,512]{2,1,0:T(8,128)(2,1)}), bf16[16,80,512]{2,1,0:T(8,128)(2,1)S(1)}, u32[]{:S(2)}, u32[]{:S(2)}) %all-to-all-start) | async-done | bytes 1310752 | tf_op jit(solution)/shard_map/all_to_all | solution.py:61
  42.5 0.1 fusion.35
  42.6 0.2 reshape_reshape_squeeze.7
  42.8 0.2 reshape_reshape_squeeze.6
  42.9 0.4 convolution_convert_fusion
  43.4 4.9 %all-to-all-start.1 = ((bf16[16,40,512]{2,1,0:T(8,128)(2,1)}), bf16[16,40,512]{2,1,0:T(8,128)(2,1)S(1)}, u32[]{:S(2)}, u32[]{:S(2)}) async-start(bf16[16,40,512]{2,1,0:T(8,128)(2,1)} %bitcast.47), calls=%async_computation.1 | async-start | bytes 1310720 | tf_op jit(solution)/shard_map/all_to_all | solution.py:78
  48.4 1.2 %fusion.31 = s32[640]{0:T(1024)S(1)} fusion(s32[]{:T(128)} %bitcast.7, s32[]{:T(128)} %bitcast.6), kind=kLoop, calls=%fused_computation.60 | loop fusion | flops 8960 | bytes 2568 | tf_op jit(solution)/shard_map/mul | solution.py:87
  49.6 4.7 %collective-permute-start = (bf16[4,128,128]{2,1,0:T(8,128)(2,1)S(1)}, bf16[4,128,128]{2,1,0:T(8,128)(2,1)S(1)}, u32[]{:S(2)}, u32[]{:S(2)}) collective-permute-start(bf16[4,128,128]{2,1,0:T(8,128)(2,1)S(1)} %broadcast_select_fusion), channel_id=1, source_target_pairs={{0,64},{16,80},{32,96},{48,112},{64,0},{80,16},{96,32},{112,48},{1... | collective-permute-start | bytes 393224 | tf_op jit(solution)/shard_map/ppermute | solution.py:14
  54.3 7.1 %collective-permute-done = bf16[4,128,128]{2,1,0:T(8,128)(2,1)S(1)} collective-permute-done((bf16[4,128,128]{2,1,0:T(8,128)(2,1)S(1)}, bf16[4,128,128]{2,1,0:T(8,128)(2,1)S(1)}, u32[]{:S(2)}, u32[]{:S(2)}) %collective-permute-start) | collective-permute-done | bytes 131104 | tf_op jit(solution)/shard_map/ppermute | solution.py:14
  61.5 5.0 %collective-permute-start.3 = (bf16[4,128,128]{2,1,0:T(8,128)(2,1)S(1)}, bf16[4,128,128]{2,1,0:T(8,128)(2,1)S(1)}, u32[]{:S(2)}, u32[]{:S(2)}) collective-permute-start(bf16[4,128,128]{2,1,0:T(8,128)(2,1)S(1)} %get-tuple-element.19), channel_id=1, source_target_pairs={{32,0},{48,16},{64,32},{80,48},{96,64},{112,80},{33,1},{49,17},{65... | collective-permute-start | bytes 393224 | tf_op jit(solution)/shard_map/ppermute | solution.py:24
  66.5 4.1 %collective-permute-start.1 = (bf16[4,128,128]{2,1,0:T(8,128)(2,1)S(1)}, bf16[4,128,128]{2,1,0:T(8,128)(2,1)S(1)}, u32[]{:S(2)}, u32[]{:S(2)}) collective-permute-start(bf16[4,128,128]{2,1,0:T(8,128)(2,1)S(1)} %get-tuple-element.20), channel_id=1, source_target_pairs={{0,32},{16,48},{32,64},{48,80},{64,96},{80,112},{1,33},{17,49},{33... | collective-permute-start | bytes 393224 | tf_op jit(solution)/shard_map/ppermute | solution.py:21
  70.7 1.1 %broadcast_compare_fusion = pred[640,640]{1,0:T(8,128)(4,1)} fusion(s32[640]{0:T(1024)S(1)} %fusion.26), kind=kLoop, calls=%fused_computation.13 | loop fusion | flops 409600 | bytes 412160 | tf_op jit(solution)/shard_map/ge | solution.py:89
  71.7 0.2 reshape_squeeze.7
  71.9 1.0 %reshape_squeeze.6 = bf16[640,4,128]{2,1,0:T(4,128)(2,1)} reshape(bf16[16,1,40,512]{3,2,1,0:T(8,128)(2,1)S(1)} %get-tuple-element.13) | data formatting | bytes 1310720 | tf_op jit(solution)/shard_map/reshape;squeeze | solution.py:64
  72.9 4.0 %collective-permute-done.1 = bf16[4,128,128]{2,1,0:T(8,128)(2,1)S(1)} collective-permute-done((bf16[4,128,128]{2,1,0:T(8,128)(2,1)S(1)}, bf16[4,128,128]{2,1,0:T(8,128)(2,1)S(1)}, u32[]{:S(2)}, u32[]{:S(2)}) %collective-permute-start.1) | collective-permute-done | bytes 131104 | tf_op jit(solution)/shard_map/ppermute | solution.py:21
  76.9 0.8 fusion.21
  77.7 5.9 %collective-permute-start.2 = (bf16[4,128,128]{2,1,0:T(8,128)(2,1)}, bf16[4,128,128]{2,1,0:T(8,128)(2,1)S(1)}, u32[]{:S(2)}, u32[]{:S(2)}) collective-permute-start(bf16[4,128,128]{2,1,0:T(8,128)(2,1)} %get-tuple-element.18), channel_id=1, source_target_pairs={{0,16},{16,32},{32,48},{48,64},{64,80},{80,96},{96,112},{1,17},{17... | collective-permute-start | bytes 393224 | tf_op jit(solution)/shard_map/ppermute | solution.py:21
  83.6 1.9 %collective-permute-start.4 = (bf16[4,128,128]{2,1,0:T(8,128)(2,1)}, bf16[4,128,128]{2,1,0:T(8,128)(2,1)S(1)}, u32[]{:S(2)}, u32[]{:S(2)}) collective-permute-start(bf16[4,128,128]{2,1,0:T(8,128)(2,1)} %get-tuple-element.17), channel_id=1, source_target_pairs={{16,0},{32,16},{48,32},{64,48},{80,64},{96,80},{112,96},{17,1},{33... | collective-permute-start | bytes 393224 | tf_op jit(solution)/shard_map/ppermute | solution.py:24
  85.6 1.0 %reshape.142 = bf16[640,4,128]{2,1,0:T(4,128)(2,1)} reshape(bf16[16,40,512]{2,1,0:T(8,128)(2,1)S(1)} %all-to-all-done.1) | data formatting | bytes 1310720 | tf_op jit(solution)/shard_map/reshape | solution.py:79
  86.6 3.4 %fusion.5 = f32[640,4,128]{0,2,1:T(8,128)S(1)} fusion(pred[640,640]{1,0:T(8,128)(4,1)} %broadcast_compare_fusion, bf16[640,4,128]{2,1,0:T(4,128)(2,1)S(1)} %reshape_squeeze.7, bf16[640,4,128]{2,1,0:T(4,128)(2,1)} %reshape.142, bf16[640,4,128]{2,1,0:T(4,128)(2,1)} %reshape_squeeze.6), kind=kOutput, calls=%fused_computation.5 | convolution fusion | flops 842137600 | bytes 3686400 | tf_op jit(solution)/shard_map/hts,she->the/dot_general | solution.py:91
  90.2 1.8 %collective-permute-done.4 = bf16[4,128,128]{2,1,0:T(8,128)(2,1)S(1)} collective-permute-done((bf16[4,128,128]{2,1,0:T(8,128)(2,1)}, bf16[4,128,128]{2,1,0:T(8,128)(2,1)S(1)}, u32[]{:S(2)}, u32[]{:S(2)}) %collective-permute-start.4) | collective-permute-done | bytes 131104 | tf_op jit(solution)/shard_map/ppermute | solution.py:24
  91.9 0.4 convolution_bitcast_fusion
  92.3 0.4 convolution_bitcast_fusion.1
  92.7 0.4 multiply_reduce_fusion
  93.1 0.3 copy-done.1
  93.4 0.4 multiply_convert_fusion
  93.8 1.1 %copy.19 = bf16[640,512]{1,0:T(8,128)(2,1)} copy(bf16[640,512]{0,1:T(8,128)(2,1)S(1)} %bitcast.49) | data formatting | bytes 1310720 | tf_op jit(solution)/shard_map/reshape | solution.py:99
  (16 shorter events, 0.4 us)
Async XLA Ops:
  2.6 7.8 %copy-start = (bf16[40,8192]{1,0:T(8,128)(2,1)S(1)}, bf16[40,8192]{1,0:T(8,128)(2,1)}, u32[]{:S(2)}) copy-start(bf16[40,8192]{1,0:T(8,128)(2,1)} %param.5) | copy-start | bytes 1966084
  2.6 39.9 %all-to-all-start = ((bf16[16,80,512]{2,1,0:T(8,128)(2,1)}), bf16[16,80,512]{2,1,0:T(8,128)(2,1)S(1)}, u32[]{:S(2)}, u32[]{:S(2)}) async-start(bf16[16,80,512]{2,1,0:T(8,128)(2,1)} %bitcast.4), calls=%async_computation | async-start | bytes 2621440 | tf_op jit(solution)/shard_map/all_to_all | solution.py:61
  10.4 0.9 copy-start.2
  43.4 42.1 %all-to-all-start.1 = ((bf16[16,40,512]{2,1,0:T(8,128)(2,1)}), bf16[16,40,512]{2,1,0:T(8,128)(2,1)S(1)}, u32[]{:S(2)}, u32[]{:S(2)}) async-start(bf16[16,40,512]{2,1,0:T(8,128)(2,1)} %bitcast.47), calls=%async_computation.1 | async-start | bytes 1310720 | tf_op jit(solution)/shard_map/all_to_all | solution.py:78
  49.6 11.8 %collective-permute-start = (bf16[4,128,128]{2,1,0:T(8,128)(2,1)S(1)}, bf16[4,128,128]{2,1,0:T(8,128)(2,1)S(1)}, u32[]{:S(2)}, u32[]{:S(2)}) collective-permute-start(bf16[4,128,128]{2,1,0:T(8,128)(2,1)S(1)} %broadcast_select_fusion), channel_id=1, source_target_pairs={{0,64},{16,80},{32,96},{48,112},{64,0},{80,16},{96,32},{112,48},{1... | collective-permute-start | bytes 393224 | tf_op jit(solution)/shard_map/ppermute | solution.py:14
  61.5 11.4 %collective-permute-start.3 = (bf16[4,128,128]{2,1,0:T(8,128)(2,1)S(1)}, bf16[4,128,128]{2,1,0:T(8,128)(2,1)S(1)}, u32[]{:S(2)}, u32[]{:S(2)}) collective-permute-start(bf16[4,128,128]{2,1,0:T(8,128)(2,1)S(1)} %get-tuple-element.19), channel_id=1, source_target_pairs={{32,0},{48,16},{64,32},{80,48},{96,64},{112,80},{33,1},{49,17},{65... | collective-permute-start | bytes 393224 | tf_op jit(solution)/shard_map/ppermute | solution.py:24
  66.5 10.4 %collective-permute-start.1 = (bf16[4,128,128]{2,1,0:T(8,128)(2,1)S(1)}, bf16[4,128,128]{2,1,0:T(8,128)(2,1)S(1)}, u32[]{:S(2)}, u32[]{:S(2)}) collective-permute-start(bf16[4,128,128]{2,1,0:T(8,128)(2,1)S(1)} %get-tuple-element.20), channel_id=1, source_target_pairs={{0,32},{16,48},{32,64},{48,80},{64,96},{80,112},{1,33},{17,49},{33... | collective-permute-start | bytes 393224 | tf_op jit(solution)/shard_map/ppermute | solution.py:21
  77.7 12.4 %collective-permute-start.2 = (bf16[4,128,128]{2,1,0:T(8,128)(2,1)}, bf16[4,128,128]{2,1,0:T(8,128)(2,1)S(1)}, u32[]{:S(2)}, u32[]{:S(2)}) collective-permute-start(bf16[4,128,128]{2,1,0:T(8,128)(2,1)} %get-tuple-element.18), channel_id=1, source_target_pairs={{0,16},{16,32},{32,48},{48,64},{64,80},{80,96},{96,112},{1,17},{17... | collective-permute-start | bytes 393224 | tf_op jit(solution)/shard_map/ppermute | solution.py:21
  83.6 8.3 %collective-permute-start.4 = (bf16[4,128,128]{2,1,0:T(8,128)(2,1)}, bf16[4,128,128]{2,1,0:T(8,128)(2,1)S(1)}, u32[]{:S(2)}, u32[]{:S(2)}) collective-permute-start(bf16[4,128,128]{2,1,0:T(8,128)(2,1)} %get-tuple-element.17), channel_id=1, source_target_pairs={{16,0},{32,16},{48,32},{64,48},{80,64},{96,80},{112,96},{17,1},{33... | collective-permute-start | bytes 393224 | tf_op jit(solution)/shard_map/ppermute | solution.py:24
  92.7 0.7 copy-start.1

commit v2 on v1

--- a/solution.py
+++ b/solution.py
@@ -9,24 +9,20 @@
 def exchange(lows, both, here, pairs):
     up = lows.astype(jnp.float32)
     down = both.astype(jnp.float32)
-    step = pairs // 2
-    msg = jnp.where(here + step < pairs, lows, both)
-    got = lax.ppermute(
-        msg, "seq", [(i, (i + step) % pairs) for i in range(pairs)]
-    ).astype(jnp.float32)
-    up = up + jnp.where(here >= step, got, 0.0)
-    down = down + jnp.where(here + step < pairs, got, 0.0)
-    step //= 2
-    while step >= 1:
-        got_up = lax.ppermute(
-            up.astype(jnp.bfloat16), "seq", [(i, i + step) for i in range(pairs - step)]
-        )
-        got_down = lax.ppermute(
-            down.astype(jnp.bfloat16), "seq", [(i, i - step) for i in range(step, pairs)]
-        )
+    got_up = lax.ppermute(lows, "seq", [(i, i + 3) for i in range(pairs - 3)])
+    got_down = lax.ppermute(both, "seq", [(i, i - 3) for i in range(3, pairs)])
+    msg = jnp.where(here + 6 < pairs, lows, both)
+    far = [(i, i + 6) for i in range(pairs - 6)] + [(i, i - 6) for i in range(6, pairs)]
+    got_far = lax.ppermute(msg, "seq", far).astype(jnp.float32)
+    up = up + got_up.astype(jnp.float32) + jnp.where(here >= 6, got_far, 0.0)
+    down = down + got_down.astype(jnp.float32) + jnp.where(here + 6 < pairs, got_far, 0.0)
+    sent_up = up.astype(jnp.bfloat16)
+    sent_down = down.astype(jnp.bfloat16)
+    for step in (1, 2):
+        got_up = lax.ppermute(sent_up, "seq", [(i, i + step) for i in range(pairs - step)])
+        got_down = lax.ppermute(sent_down, "seq", [(i, i - step) for i in range(step, pairs)])
         up = up + got_up.astype(jnp.float32)
         down = down + got_down.astype(jnp.float32)
-        step //= 2
     low_sum = up - lows.astype(jnp.float32)
     high_sum = low_sum + (down - both.astype(jnp.float32))
     return low_sum, high_sum

time: 95.4 us -> 97.4 us (1.021)
  the two profiles are of different devices: /device:TPU:902 before, /device:TPU:6 now
where the time goes in v2:
time: 97.4 us; the launch traced here: 96.8 us
  starting transfers between devices  39.7 us (41%)
  waiting for transfers between devices  37.6 us (39%)
  local copies, waits for them, and re-layouts  6.96 us (7%)
  matrix products  6.57 us (7%)
  other arithmetic  5.17 us (5%)
    all_to_all x1, waiting for transfers between devices, local(): kv_all = lax.all_to_all(kv, 'head', split_axis=0, concat_axis=0, tiled=True)  30 us
    ppermute x1, starting transfers between devices, exchange(): got_down = lax.ppermute(both, 'seq', [(i, i - 3) for i in range(3, pairs)])  11 us
    ppermute x2, starting transfers between devices, exchange(): lax.ppermute(sent_up, 'seq', [(i, i + step) for i in range(pairs - step)])  8.92 us
    all_to_all x1, starting transfers between devices, local(): kv_all = lax.all_to_all(kv, 'head', split_axis=0, concat_axis=0, tiled=True)  7.79 us
    all_to_all x1, starting transfers between devices, local(): lax.all_to_all(q_in, 'head', split_axis=0, concat_axis=0, tiled=True)  4.92 us
    ppermute x1, waiting for transfers between devices, exchange(): got_up = lax.ppermute(lows, 'seq', [(i, i + 3) for i in range(pairs - 3)])  4.92 us
    ppermute x2, starting transfers between devices, exchange(): lax.ppermute(sent_down, 'seq', [(i, i - step) for i in range(step, pairs)])  4.49 us
    dot_general x1, matrix products, local(): jnp.einsum('hts,she->the', scores, vx, preferred_element_type=jnp.float32)  3.36 us
  transfers between devices with their start and end apart: 9, of which 5 were waited for; matrix products, arithmetic and copies ran while one was open for 11% of the time, Pallas kernels for 0%

profile of v2, /device:TPU:6, one launch (start us, length us, event | category | flops | bytes accessed | tf_op | source)
XLA Modules:
  0.0 96.8 jit_solution(4061920166128627167)
XLA Ops:
  0.0 1.4 %bitcast_bitcast_fusion.1 = (bf16[16,1,40,512]{3,2,1,0:T(8,128)(2,1)S(1)}, bf16[16,1,40,512]{3,2,1,0:T(8,128)(2,1)S(1)}) fusion(bf16[5,16,8,512]{3,2,1,0:T(8,128)(2,1)} %bitcast.50, bf16[5,16,8,512]{3,2,1,0:T(8,128)(2,1)} %bitcast.51), kind=kLoop, calls=%fused_computation.15 | loop fusion | bytes 2621440 | tf_op jit(solution)/shard_map/stack;squeeze;reshape | solution.py:53
  1.4 1.2 %pad_maximum_fusion = bf16[16,2,40,512]{3,2,1,0:T(8,128)(2,1)} fusion(bf16[16,1,40,512]{3,2,1,0:T(8,128)(2,1)S(1)} %get-tuple-element.21, bf16[16,1,40,512]{3,2,1,0:T(8,128)(2,1)S(1)} %get-tuple-element.22), kind=kLoop, calls=%fused_computation.6 | loop fusion | flops 655360 | bytes 2621440 | tf_op jit(solution)/shard_map/stack | solution.py:53
  2.6 7.8 %all-to-all-start = ((bf16[16,80,512]{2,1,0:T(8,128)(2,1)}), bf16[16,80,512]{2,1,0:T(8,128)(2,1)S(1)}, u32[]{:S(2)}, u32[]{:S(2)}) async-start(bf16[16,80,512]{2,1,0:T(8,128)(2,1)} %bitcast.4), calls=%async_computation | async-start | bytes 2621440 | tf_op jit(solution)/shard_map/all_to_all | solution.py:57
  10.4 0.9 copy.46
  11.3 0.6 fusion.35
  12.5 30.0 %all-to-all-done = bf16[16,80,512]{2,1,0:T(8,128)(2,1)S(1)} async-done(((bf16[16,80,512]{2,1,0:T(8,128)(2,1)}), bf16[16,80,512]{2,1,0:T(8,128)(2,1)S(1)}, u32[]{:S(2)}, u32[]{:S(2)}) %all-to-all-start) | async-done | bytes 1310752 | tf_op jit(solution)/shard_map/all_to_all | solution.py:57
  42.6 0.2 reshape_reshape_squeeze.7
  42.9 0.4 convolution_convert_fusion
  43.4 4.9 %all-to-all-start.1 = ((bf16[16,40,512]{2,1,0:T(8,128)(2,1)}), bf16[16,40,512]{2,1,0:T(8,128)(2,1)S(1)}, u32[]{:S(2)}, u32[]{:S(2)}) async-start(bf16[16,40,512]{2,1,0:T(8,128)(2,1)} %bitcast.47), calls=%async_computation.1 | async-start | bytes 1310720 | tf_op jit(solution)/shard_map/all_to_all | solution.py:74
  48.4 1.2 %fusion.31 = s32[640]{0:T(1024)S(1)} fusion(s32[]{:T(128)} %bitcast.7, s32[]{:T(128)} %bitcast.6), kind=kLoop, calls=%fused_computation.58 | loop fusion | flops 8960 | bytes 2568 | tf_op jit(solution)/shard_map/mul | solution.py:83
  49.6 11.0 %collective-permute-start.4 = (bf16[4,128,128]{2,1,0:T(8,128)(2,1)S(1)}, bf16[4,128,128]{2,1,0:T(8,128)(2,1)S(1)}, u32[]{:S(2)}, u32[]{:S(2)}) collective-permute-start(bf16[4,128,128]{2,1,0:T(8,128)(2,1)S(1)} %get-tuple-element.10), channel_id=1, source_target_pairs={{48,0},{64,16},{80,32},{96,48},{112,64},{49,1},{65,17},{81,33},{97... | collective-permute-start | bytes 393224 | tf_op jit(solution)/shard_map/ppermute | solution.py:13
  60.6 1.9 %collective-permute-start = (bf16[4,128,128]{2,1,0:T(8,128)(2,1)S(1)}, bf16[4,128,128]{2,1,0:T(8,128)(2,1)S(1)}, u32[]{:S(2)}, u32[]{:S(2)}) collective-permute-start(bf16[4,128,128]{2,1,0:T(8,128)(2,1)S(1)} %get-tuple-element.9), channel_id=1, source_target_pairs={{0,48},{16,64},{32,80},{48,96},{64,112},{1,49},{17,65},{33,81},{49... | collective-permute-start | bytes 393224 | tf_op jit(solution)/shard_map/ppermute | solution.py:12
  62.5 0.7 collective-permute-start.1
  63.2 1.1 %broadcast_compare_fusion = pred[640,640]{1,0:T(8,128)(4,1)} fusion(s32[640]{0:T(1024)S(1)} %fusion.26), kind=kLoop, calls=%fused_computation.13 | loop fusion | flops 409600 | bytes 412160 | tf_op jit(solution)/shard_map/ge | solution.py:85
  64.4 1.0 %reshape_squeeze.6 = bf16[640,4,128]{2,1,0:T(4,128)(2,1)} reshape(bf16[16,1,40,512]{3,2,1,0:T(8,128)(2,1)S(1)} %get-tuple-element.13) | data formatting | bytes 1310720 | tf_op jit(solution)/shard_map/reshape;squeeze | solution.py:60
  65.4 0.2 collective-permute-done.4
  65.6 4.9 %collective-permute-done = bf16[4,128,128]{2,1,0:T(8,128)(2,1)S(1)} collective-permute-done((bf16[4,128,128]{2,1,0:T(8,128)(2,1)S(1)}, bf16[4,128,128]{2,1,0:T(8,128)(2,1)S(1)}, u32[]{:S(2)}, u32[]{:S(2)}) %collective-permute-start) | collective-permute-done | bytes 131104 | tf_op jit(solution)/shard_map/ppermute | solution.py:12
  70.6 0.8 fusion.20
  71.4 1.9 %collective-permute-start.3 = (bf16[4,128,128]{2,1,0:T(8,128)(2,1)}, bf16[4,128,128]{2,1,0:T(8,128)(2,1)S(1)}, u32[]{:S(2)}, u32[]{:S(2)}) collective-permute-start(bf16[4,128,128]{2,1,0:T(8,128)(2,1)} %get-tuple-element.18), channel_id=1, source_target_pairs={{0,32},{16,48},{32,64},{48,80},{64,96},{80,112},{1,33},{17,49},{33... | collective-permute-start | bytes 393224 | tf_op jit(solution)/shard_map/ppermute | solution.py:22
  73.3 7.0 %collective-permute-start.2 = (bf16[4,128,128]{2,1,0:T(8,128)(2,1)}, bf16[4,128,128]{2,1,0:T(8,128)(2,1)S(1)}, u32[]{:S(2)}, u32[]{:S(2)}) collective-permute-start(bf16[4,128,128]{2,1,0:T(8,128)(2,1)} %get-tuple-element.18), channel_id=1, source_target_pairs={{0,16},{16,32},{32,48},{48,64},{64,80},{80,96},{96,112},{1,17},{17... | collective-permute-start | bytes 393224 | tf_op jit(solution)/shard_map/ppermute | solution.py:22
  80.3 1.9 %collective-permute-start.6 = (bf16[4,128,128]{2,1,0:T(8,128)(2,1)}, bf16[4,128,128]{2,1,0:T(8,128)(2,1)}, u32[]{:S(2)}, u32[]{:S(2)}) collective-permute-start(bf16[4,128,128]{2,1,0:T(8,128)(2,1)} %get-tuple-element.17), channel_id=1, source_target_pairs={{32,0},{48,16},{64,32},{80,48},{96,64},{112,80},{33,1},{49,17},{65... | collective-permute-start | bytes 393224 | tf_op jit(solution)/shard_map/ppermute | solution.py:23
  82.2 2.6 %collective-permute-start.5 = (bf16[4,128,128]{2,1,0:T(8,128)(2,1)}, bf16[4,128,128]{2,1,0:T(8,128)(2,1)}, u32[]{:S(2)}, u32[]{:S(2)}) collective-permute-start(bf16[4,128,128]{2,1,0:T(8,128)(2,1)} %get-tuple-element.17), channel_id=1, source_target_pairs={{16,0},{32,16},{48,32},{64,48},{80,64},{96,80},{112,96},{17,1},{33... | collective-permute-start | bytes 393224 | tf_op jit(solution)/shard_map/ppermute | solution.py:23
  84.8 1.0 %reshape.142 = bf16[640,4,128]{2,1,0:T(4,128)(2,1)} reshape(bf16[16,40,512]{2,1,0:T(8,128)(2,1)S(1)} %all-to-all-done.1) | data formatting | bytes 1310720 | tf_op jit(solution)/shard_map/reshape | solution.py:75
  85.8 3.4 %fusion.5 = f32[640,4,128]{0,2,1:T(8,128)S(1)} fusion(pred[640,640]{1,0:T(8,128)(4,1)} %broadcast_compare_fusion, bf16[640,4,128]{2,1,0:T(4,128)(2,1)S(1)} %reshape_squeeze.7, bf16[640,4,128]{2,1,0:T(4,128)(2,1)} %reshape.142, bf16[640,4,128]{2,1,0:T(4,128)(2,1)} %reshape_squeeze.6), kind=kOutput, calls=%fused_computation.5 | convolution fusion | flops 842137600 | bytes 3686400 | tf_op jit(solution)/shard_map/hts,she->the/dot_general | solution.py:87
  89.4 2.1 %collective-permute-done.6 = bf16[4,128,128]{2,1,0:T(8,128)(2,1)} collective-permute-done((bf16[4,128,128]{2,1,0:T(8,128)(2,1)}, bf16[4,128,128]{2,1,0:T(8,128)(2,1)}, u32[]{:S(2)}, u32[]{:S(2)}) %collective-permute-start.6) | collective-permute-done | bytes 131104 | tf_op jit(solution)/shard_map/ppermute | solution.py:23
  91.6 0.3 collective-permute-done.5
  91.8 1.4 %convolution_bitcast_fusion = f32[320,4,128]{0,2,1:T(8,128)S(1)} fusion(bf16[320,4,128]{2,1,0:T(4,128)(2,1)S(1)} %squeeze.16, pred[]{:T(512)} %bitcast.9, bf16[4,128,128]{2,1,0:T(8,128)(2,1)S(1)} %get-tuple-element.9, bf16[4,128,128]{2,1,0:T(8,128)(2,1)S(1)} %collective-permute-done.3, bf16[4,128,128]{2,1,0:T(8,128)(2,1)S(1)} %collective-permute-done.2, ...), kind=kOutput, calls=%fused_computation.10 | convolution fusion | flops 43515904 | bytes 2162691 | tf_op jit(solution)/shard_map/thd,hde->the/dot_general | solution.py:91
  93.2 1.4 %convolution_bitcast_fusion.1 = f32[320,4,128]{0,2,1:T(8,128)S(1)} fusion(bf16[320,4,128]{2,1,0:T(4,128)(2,1)S(1)} %squeeze.7, pred[]{:T(512)} %bitcast.9, bf16[4,128,128]{2,1,0:T(8,128)(2,1)S(1)} %get-tuple-element.9, bf16[4,128,128]{2,1,0:T(8,128)(2,1)S(1)} %collective-permute-done.3, bf16[4,128,128]{2,1,0:T(8,128)(2,1)S(1)} %collective-permute-done.2, ...), kind=kOutput, calls=%fused_computation.11 | convolution fusion | flops 43515904 | bytes 2162691 | tf_op jit(solution)/shard_map/thd,hde->the/dot_general | solution.py:90
  94.6 0.4 multiply_reduce_fusion
  95.0 0.3 copy-done.1
  95.3 0.4 multiply_convert_fusion
  95.7 1.1 %copy.19 = bf16[640,512]{1,0:T(8,128)(2,1)} copy(bf16[640,512]{0,1:T(8,128)(2,1)S(1)} %bitcast.49) | data formatting | bytes 1310720 | tf_op jit(solution)/shard_map/reshape | solution.py:95
  (19 shorter events, 0.7 us)
Async XLA Ops:
  2.6 7.8 %copy-start = (bf16[40,8192]{1,0:T(8,128)(2,1)S(1)}, bf16[40,8192]{1,0:T(8,128)(2,1)}, u32[]{:S(2)}) copy-start(bf16[40,8192]{1,0:T(8,128)(2,1)} %param.5) | copy-start | bytes 1966084
  2.6 39.9 %all-to-all-start = ((bf16[16,80,512]{2,1,0:T(8,128)(2,1)}), bf16[16,80,512]{2,1,0:T(8,128)(2,1)S(1)}, u32[]{:S(2)}, u32[]{:S(2)}) async-start(bf16[16,80,512]{2,1,0:T(8,128)(2,1)} %bitcast.4), calls=%async_computation | async-start | bytes 2621440 | tf_op jit(solution)/shard_map/all_to_all | solution.py:57
  10.4 0.9 copy-start.2
  43.4 41.4 %all-to-all-start.1 = ((bf16[16,40,512]{2,1,0:T(8,128)(2,1)}), bf16[16,40,512]{2,1,0:T(8,128)(2,1)S(1)}, u32[]{:S(2)}, u32[]{:S(2)}) async-start(bf16[16,40,512]{2,1,0:T(8,128)(2,1)} %bitcast.47), calls=%async_computation.1 | async-start | bytes 1310720 | tf_op jit(solution)/shard_map/all_to_all | solution.py:74
  49.6 16.0 %collective-permute-start.4 = (bf16[4,128,128]{2,1,0:T(8,128)(2,1)S(1)}, bf16[4,128,128]{2,1,0:T(8,128)(2,1)S(1)}, u32[]{:S(2)}, u32[]{:S(2)}) collective-permute-start(bf16[4,128,128]{2,1,0:T(8,128)(2,1)S(1)} %get-tuple-element.10), channel_id=1, source_target_pairs={{48,0},{64,16},{80,32},{96,48},{112,64},{49,1},{65,17},{81,33},{97... | collective-permute-start | bytes 393224 | tf_op jit(solution)/shard_map/ppermute | solution.py:13
  60.6 10.0 %collective-permute-start = (bf16[4,128,128]{2,1,0:T(8,128)(2,1)S(1)}, bf16[4,128,128]{2,1,0:T(8,128)(2,1)S(1)}, u32[]{:S(2)}, u32[]{:S(2)}) collective-permute-start(bf16[4,128,128]{2,1,0:T(8,128)(2,1)S(1)} %get-tuple-element.9), channel_id=1, source_target_pairs={{0,48},{16,64},{32,80},{48,96},{64,112},{1,49},{17,65},{33,81},{49... | collective-permute-start | bytes 393224 | tf_op jit(solution)/shard_map/ppermute | solution.py:12
  62.5 2.9 %collective-permute-start.1 = (bf16[4,128,128]{2,1,0:T(8,128)(2,1)S(1)}, bf16[4,128,128]{2,1,0:T(8,128)(2,1)S(1)}, u32[]{:S(2)}, u32[]{:S(2)}) collective-permute-start(bf16[4,128,128]{2,1,0:T(8,128)(2,1)S(1)} %broadcast_select_fusion), channel_id=1, source_target_pairs={{0,96},{16,112},{96,0},{112,16},{1,97},{17,113},{97,1},{113,17},{2... | collective-permute-start | bytes 393224 | tf_op jit(solution)/shard_map/ppermute | solution.py:16
  71.4 18.0 %collective-permute-start.3 = (bf16[4,128,128]{2,1,0:T(8,128)(2,1)}, bf16[4,128,128]{2,1,0:T(8,128)(2,1)S(1)}, u32[]{:S(2)}, u32[]{:S(2)}) collective-permute-start(bf16[4,128,128]{2,1,0:T(8,128)(2,1)} %get-tuple-element.18), channel_id=1, source_target_pairs={{0,32},{16,48},{32,64},{48,80},{64,96},{80,112},{1,33},{17,49},{33... | collective-permute-start | bytes 393224 | tf_op jit(solution)/shard_map/ppermute | solution.py:22
  73.3 16.1 %collective-permute-start.2 = (bf16[4,128,128]{2,1,0:T(8,128)(2,1)}, bf16[4,128,128]{2,1,0:T(8,128)(2,1)S(1)}, u32[]{:S(2)}, u32[]{:S(2)}) collective-permute-start(bf16[4,128,128]{2,1,0:T(8,128)(2,1)} %get-tuple-element.18), channel_id=1, source_target_pairs={{0,16},{16,32},{32,48},{48,64},{64,80},{80,96},{96,112},{1,17},{17... | collective-permute-start | bytes 393224 | tf_op jit(solution)/shard_map/ppermute | solution.py:22
  80.3 11.2 %collective-permute-start.6 = (bf16[4,128,128]{2,1,0:T(8,128)(2,1)}, bf16[4,128,128]{2,1,0:T(8,128)(2,1)}, u32[]{:S(2)}, u32[]{:S(2)}) collective-permute-start(bf16[4,128,128]{2,1,0:T(8,128)(2,1)} %get-tuple-element.17), channel_id=1, source_target_pairs={{32,0},{48,16},{64,32},{80,48},{96,64},{112,80},{33,1},{49,17},{65... | collective-permute-start | bytes 393224 | tf_op jit(solution)/shard_map/ppermute | solution.py:23
  82.2 9.6 %collective-permute-start.5 = (bf16[4,128,128]{2,1,0:T(8,128)(2,1)}, bf16[4,128,128]{2,1,0:T(8,128)(2,1)}, u32[]{:S(2)}, u32[]{:S(2)}) collective-permute-start(bf16[4,128,128]{2,1,0:T(8,128)(2,1)} %get-tuple-element.17), channel_id=1, source_target_pairs={{16,0},{32,16},{48,32},{64,48},{80,64},{96,80},{112,96},{17,1},{33... | collective-permute-start | bytes 393224 | tf_op jit(solution)/shard_map/ppermute | solution.py:23
  94.6 0.7 copy-start.1
